TPU v7x, 256 devices: a whole 4x4x8 slice. The times are simulated.
256 devices in a mesh: space: 64 (over x, y, z_hi), chan: 4 (over z_lo, core).
Axes of the slice: x: 4, y: 4, z: 8 (z_hi: 4, z_lo: 2; z = z_hi * 2 + z_lo), core: 2. Of those that a mesh axis runs over, the one named last changes fastest.
Arguments:
- voxels: bfloat16 [32, 128, 16, 512], P(None, 'space'), may hold values from -6 to 6
- first_filters: bfloat16 [3, 3, 3, 64, 32], P(None, None, None, 'chan'), may hold values from -0.21875 to 0.21875
- second_filters: bfloat16 [3, 3, 3, 64, 64], P(None, None, None, 'chan'), may hold values from -0.15625 to 0.15625
Outputs:
- filtered: bfloat16 [64, 128, 16, 512], P('chan', 'space')
All inputs are finite; a program needn't handle non-finite values.
Results may differ from a plain program's by a relative error of at most 0.0049.
Values may be sent and summed in bfloat16 or wider, within the bound.
No kernel may reach another device: no remote copies, remote signals or barrier semaphores. Data moves between devices by JAX's collectives and lax.ppermute only.
A program may use at most 64 MiB of HBM per device.

v0:
```python
import jax
import jax.numpy as jnp
from jax import lax
from jax.sharding import PartitionSpec as P

GH = 8


def passed_along(value, axis, steps):
    count = lax.axis_size(axis)
    pairs = [(source, (source + steps) % count) for source in range(count)]
    return lax.ppermute(value, axis, pairs)


def widen(volume_tile):
    zero_col = jnp.zeros(volume_tile.shape[:3] + (1,), volume_tile.dtype)
    left_shift = jnp.concatenate([zero_col, volume_tile[..., :-1]], 3)
    right_shift = jnp.concatenate([volume_tile[..., 1:], zero_col], 3)
    return jnp.concatenate([left_shift, volume_tile, right_shift], 0)


def tile_border(volume_tile, above, below, front, back):
    tile_count = lax.axis_size("space")
    position = (lax.axis_index("space") + GH + GH // 4) % tile_count
    tile_row = position % GH
    depth_tile = position // GH
    grid_depth = tile_count // GH
    above_rim = above(volume_tile[:, :, -1:, :])
    below_rim = below(volume_tile[:, :, :1, :])
    above_rim = jnp.where(tile_row > 0, above_rim, jnp.zeros_like(above_rim))
    below_rim = jnp.where(tile_row < GH - 1, below_rim, jnp.zeros_like(below_rim))
    taller = jnp.concatenate([above_rim, volume_tile, below_rim], 2)
    front_rim = front(taller[:, -1:])
    back_rim = back(taller[:, :1])
    front_rim = jnp.where(depth_tile > 0, front_rim, jnp.zeros_like(front_rim))
    back_rim = jnp.where(depth_tile < grid_depth - 1, back_rim, jnp.zeros_like(back_rim))
    return jnp.concatenate([front_rim, taller, back_rim], 1)


def input_above(rim_cells):
    return passed_along(rim_cells, "space", 1)


def input_below(rim_cells):
    return passed_along(rim_cells, "space", -1)


def input_front(rim_cells):
    return passed_along(rim_cells, "space", GH)


def input_back(rim_cells):
    return passed_along(rim_cells, "space", -GH)


def hidden_above(rim_cells):
    return passed_along(rim_cells, "space", 1)


def hidden_below(rim_cells):
    return passed_along(rim_cells, "space", -1)


def hidden_front(rim_cells):
    return passed_along(rim_cells, "space", GH)


def hidden_back(rim_cells):
    return passed_along(rim_cells, "space", -GH)


def correlate(stacked, filters, depth_rows, height_rows):
    out_count = filters.shape[3]
    running = jnp.zeros((out_count, depth_rows, height_rows, stacked.shape[3]), jnp.float32)
    for depth_tap in range(3):
        for height_tap in range(3):
            matrix = filters[depth_tap, height_tap].transpose(1, 0, 2).reshape(out_count, -1)
            window = stacked[
                :, depth_tap : depth_tap + depth_rows, height_tap : height_tap + height_rows, :
            ]
            running = running + jnp.einsum(
                "ok,kdhw->odhw", matrix, window, preferred_element_type=jnp.float32
            )
    return running


def local(voxels, first_filters, second_filters):
    depth_rows = voxels.shape[1]
    height_rows = voxels.shape[2]
    padded = tile_border(voxels, input_above, input_below, input_front, input_back)
    hidden = jax.nn.relu(correlate(widen(padded), first_filters, depth_rows, height_rows)).astype(
        jnp.bfloat16
    )
    hidden_pad = tile_border(hidden, hidden_above, hidden_below, hidden_front, hidden_back)
    summed = correlate(
        widen(lax.all_gather(hidden_pad, "chan", axis=0, tiled=True)),
        second_filters,
        depth_rows,
        height_rows,
    )
    return jax.nn.relu(summed).astype(jnp.bfloat16)


def solution(mesh):
    return jax.shard_map(
        local,
        mesh=mesh,
        in_specs=(
            P(None, "space", None, None),
            P(None, None, None, "chan", None),
            P(None, None, None, "chan", None),
        ),
        out_specs=P("chan", "space", None, None),
        check_vma=False,
    )
```

profile of v0, /device:TPU:1, one launch (start us, length us, event | category | flops | bytes accessed | tf_op | source)
XLA Modules:
  0.0 173.7 jit_solution(5258099566370104163)
XLA Ops:
  6.5 1.8 %copy.26 = bf16[32,2,16,512]{3,0,2,1:T(8,128)(2,1)S(1)} copy(bf16[32,2,16,512]{3,2,1,0:T(8,128)(2,1)} %param.3) | data formatting | bytes 2097152 | tf_op args[0]
  8.4 3.9 %collective-permute-start = (bf16[32,2,1,512]{3,0,2,1:T(8,128)(2,1)S(1)}, bf16[32,2,1,512]{3,0,2,1:T(8,128)(2,1)S(1)}, u32[]{:S(2)}, u32[]{:S(2)}) collective-permute-start(bf16[32,2,1,512]{3,0,2,1:T(8,128)(2,1)S(1)} %get-tuple-element.11), channel_id=1, source_target_pairs={{0,4},{4,8},{8,12},{12,16},{16,20},{20,24},{24,28},{28,32},{32,36}... | collective-permute-start | bytes 196616 | tf_op jit(solution)/shard_map/ppermute | solution.py:12
  12.2 7.8 %collective-permute-start.1 = (bf16[32,2,1,512]{3,0,2,1:T(8,128)(2,1)S(1)}, bf16[32,2,1,512]{3,0,2,1:T(8,128)(2,1)S(1)}, u32[]{:S(2)}, u32[]{:S(2)}) collective-permute-start(bf16[32,2,1,512]{3,0,2,1:T(8,128)(2,1)S(1)} %get-tuple-element.12), channel_id=1, source_target_pairs={{0,252},{4,0},{8,4},{12,8},{16,12},{20,16},{24,20},{28,24},{32,28}... | collective-permute-start | bytes 196616 | tf_op jit(solution)/shard_map/ppermute | solution.py:12
  20.0 1.7 collective-permute-done
  22.5 4.6 %collective-permute-start.3 = (bf16[32,1,18,512]{3,0,2,1:T(8,128)(2,1)S(1)}, bf16[32,1,18,512]{3,0,2,1:T(8,128)(2,1)S(1)}, u32[]{:S(2)}, u32[]{:S(2)}) collective-permute-start(bf16[32,1,18,512]{3,0,2,1:T(8,128)(2,1)S(1)} %get-tuple-element.10), channel_id=1, source_target_pairs={{0,224},{4,228},{8,232},{12,236},{16,240},{20,244},{24,248},{28,25... | collective-permute-start | bytes 1769480 | tf_op jit(solution)/shard_map/ppermute | solution.py:12
  27.1 1.5 slice_bitcast_fusion.17
  29.3 0.7 copy.36
  30.7 0.7 copy.35
  40.4 5.7 %collective-permute-done.2 = bf16[32,1,18,512]{3,0,2,1:T(8,128)(2,1)S(1)} collective-permute-done((bf16[32,1,18,512]{3,0,2,1:T(8,128)(2,1)S(1)}, bf16[32,1,18,512]{3,0,2,1:T(8,128)(2,1)S(1)}, u32[]{:S(2)}, u32[]{:S(2)}) %collective-permute-start.2) | collective-permute-done | bytes 589856 | tf_op jit(solution)/shard_map/ppermute | solution.py:12
  46.2 4.0 %collective-permute-done.3 = bf16[32,1,18,512]{3,0,2,1:T(8,128)(2,1)S(1)} collective-permute-done((bf16[32,1,18,512]{3,0,2,1:T(8,128)(2,1)S(1)}, bf16[32,1,18,512]{3,0,2,1:T(8,128)(2,1)S(1)}, u32[]{:S(2)}, u32[]{:S(2)}) %collective-permute-start.3) | collective-permute-done | bytes 589856 | tf_op jit(solution)/shard_map/ppermute | solution.py:12
  50.7 1.6 fusion.129
  52.3 2.9 %fusion.6 = bf16[96,4,18,512]{3,0,2,1:T(8,128)(2,1)S(1)} fusion(bf16[32,4,18,511]{3,0,2,1:T(8,128)(2,1)S(1)} %get-tuple-element.8, bf16[32,4,18,511]{3,0,2,1:T(8,128)(2,1)S(1)} %get-tuple-element.7, bf16[32,1,18,512]{3,0,2,1:T(8,128)(2,1)S(1)} %broadcast_select_fusion, bf16[32,2,1,512]{3,0,2,1:T(8,128)(2,1)S(1)} %broadcast_select_fusion.4, ...), kind=kLoop, calls=%fused_computation.10 | loop fusion | flops 63700992 | bytes 14146560 | tf_op jit(solution)/shard_map/concatenate | solution.py:19
  60.2 4.0 %collective-permute-start.4 = (bf16[16,2,1,512]{3,0,2,1:T(8,128)(2,1)S(1)}, bf16[16,2,1,512]{3,0,2,1:T(8,128)(2,1)S(1)}, u32[]{:S(2)}, u32[]{:S(2)}) collective-permute-start(bf16[16,2,1,512]{3,0,2,1:T(8,128)(2,1)S(1)} %get-tuple-element.15), channel_id=1, source_target_pairs={{0,4},{4,8},{8,12},{12,16},{16,20},{20,24},{24,28},{28,32},{32,36}... | collective-permute-start | bytes 98312 | tf_op jit(solution)/shard_map/ppermute | solution.py:12
  64.1 4.5 %collective-permute-start.5 = (bf16[16,2,1,512]{3,0,2,1:T(8,128)(2,1)S(1)}, bf16[16,2,1,512]{3,0,2,1:T(8,128)(2,1)S(1)}, u32[]{:S(2)}, u32[]{:S(2)}) collective-permute-start(bf16[16,2,1,512]{3,0,2,1:T(8,128)(2,1)S(1)} %get-tuple-element.16), channel_id=1, source_target_pairs={{0,252},{4,0},{8,4},{12,8},{16,12},{20,16},{24,20},{28,24},{32,28}... | collective-permute-start | bytes 98312 | tf_op jit(solution)/shard_map/ppermute | solution.py:12
  68.6 1.0 collective-permute-done.4
  69.9 5.1 %collective-permute-start.7 = (bf16[16,1,18,512]{3,0,2,1:T(8,128)(2,1)S(1)}, bf16[16,1,18,512]{3,0,2,1:T(8,128)(2,1)S(1)}, u32[]{:S(2)}, u32[]{:S(2)}) collective-permute-start(bf16[16,1,18,512]{3,0,2,1:T(8,128)(2,1)S(1)} %get-tuple-element.14), channel_id=1, source_target_pairs={{0,224},{4,228},{8,232},{12,236},{16,240},{20,244},{24,248},{28,25... | collective-permute-start | bytes 884744 | tf_op jit(solution)/shard_map/ppermute | solution.py:12
  75.0 4.2 %collective-permute-done.6 = bf16[16,1,18,512]{3,0,2,1:T(8,128)(2,1)S(1)} collective-permute-done((bf16[16,1,18,512]{3,0,2,1:T(8,128)(2,1)S(1)}, bf16[16,1,18,512]{3,0,2,1:T(8,128)(2,1)S(1)}, u32[]{:S(2)}, u32[]{:S(2)}) %collective-permute-start.6) | collective-permute-done | bytes 294944 | tf_op jit(solution)/shard_map/ppermute | solution.py:12
  79.2 5.5 %collective-permute-done.7 = bf16[16,1,18,512]{3,0,2,1:T(8,128)(2,1)S(1)} collective-permute-done((bf16[16,1,18,512]{3,0,2,1:T(8,128)(2,1)S(1)}, bf16[16,1,18,512]{3,0,2,1:T(8,128)(2,1)S(1)}, u32[]{:S(2)}, u32[]{:S(2)}) %collective-permute-start.7) | collective-permute-done | bytes 294944 | tf_op jit(solution)/shard_map/ppermute | solution.py:12
  84.8 1.2 pad_maximum_fusion.2
  86.9 54.6 %all-gather.2.cloned.1.call-done = bf16[64,4,18,512]{3,0,2,1:T(8,128)(2,1)} async-done(((bf16[16,4,18,512]{3,0,2,1:T(8,128)(2,1)}), bf16[64,4,18,512]{3,0,2,1:T(8,128)(2,1)}) %all-gather.2.cloned.1.call-update) | async-done | bytes 4718608 | tf_op jit(solution)/shard_map/all_gather | solution.py:96
  141.6 9.0 %fusion.128 = (bf16[64,4,18,511]{3,0,2,1:T(8,128)(2,1)S(1)}, bf16[64,4,18,511]{3,0,2,1:T(8,128)(2,1)}) fusion(bf16[64,4,18,512]{3,0,2,1:T(8,128)(2,1)} %all-gather.2.cloned.1.call-done), kind=kLoop, calls=%fused_computation.118 | loop fusion | bytes 18837504 | tf_op jit(solution)/shard_map/slice | solution.py:17
  150.6 6.7 %fusion.2 = bf16[192,4,18,512]{3,0,2,1:T(8,128)(2,1)S(1)} fusion(bf16[64,4,18,511]{3,0,2,1:T(8,128)(2,1)} %get-tuple-element.6, bf16[64,4,18,511]{3,0,2,1:T(8,128)(2,1)S(1)} %get-tuple-element.5, bf16[64,4,18,512]{3,0,2,1:T(8,128)(2,1)S(1)} %copy-done), kind=kLoop, calls=%fused_computation.4 | loop fusion | flops 70778880 | bytes 28293120 | tf_op jit(solution)/shard_map/concatenate | solution.py:19
  157.3 0.9 fusion.22
  158.2 0.9 fusion.59
  159.2 0.9 fusion.62
  160.1 0.9 fusion.65
  161.1 0.9 fusion.68
  162.0 0.9 fusion.71
  162.9 0.9 fusion.74
  163.9 0.9 fusion.77
  164.8 0.9 fusion.107
  165.7 1.1 copy.47
  (87 shorter events, 17.8 us)
Async XLA Ops:
  6.5 135.0 %all-gather.2.cloned.1.call-start = ((), (), s32[]{:S(2)}) async-start(), calls=%async_computation | async-start | bytes 5898240 | tf_op jit(solution)/shard_map/all_gather | solution.py:96
  8.4 13.3 %collective-permute-start = (bf16[32,2,1,512]{3,0,2,1:T(8,128)(2,1)S(1)}, bf16[32,2,1,512]{3,0,2,1:T(8,128)(2,1)S(1)}, u32[]{:S(2)}, u32[]{:S(2)}) collective-permute-start(bf16[32,2,1,512]{3,0,2,1:T(8,128)(2,1)S(1)} %get-tuple-element.11), channel_id=1, source_target_pairs={{0,4},{4,8},{8,12},{12,16},{16,20},{20,24},{24,28},{28,32},{32,36}... | collective-permute-start | bytes 196616 | tf_op jit(solution)/shard_map/ppermute | solution.py:12
  12.2 9.4 %collective-permute-start.1 = (bf16[32,2,1,512]{3,0,2,1:T(8,128)(2,1)S(1)}, bf16[32,2,1,512]{3,0,2,1:T(8,128)(2,1)S(1)}, u32[]{:S(2)}, u32[]{:S(2)}) collective-permute-start(bf16[32,2,1,512]{3,0,2,1:T(8,128)(2,1)S(1)} %get-tuple-element.12), channel_id=1, source_target_pairs={{0,252},{4,0},{8,4},{12,8},{16,12},{20,16},{24,20},{28,24},{32,28}... | collective-permute-start | bytes 196616 | tf_op jit(solution)/shard_map/ppermute | solution.py:12
  22.0 24.2 %collective-permute-start.2 = (bf16[32,1,18,512]{3,0,2,1:T(8,128)(2,1)S(1)}, bf16[32,1,18,512]{3,0,2,1:T(8,128)(2,1)S(1)}, u32[]{:S(2)}, u32[]{:S(2)}) collective-permute-start(bf16[32,1,18,512]{3,0,2,1:T(8,128)(2,1)S(1)} %get-tuple-element.9), channel_id=1, source_target_pairs={{0,32},{4,36},{8,40},{12,44},{16,48},{20,52},{24,56},{28,60},{32,6... | collective-permute-start | bytes 1769480 | tf_op jit(solution)/shard_map/ppermute | solution.py:12
  22.5 27.7 %collective-permute-start.3 = (bf16[32,1,18,512]{3,0,2,1:T(8,128)(2,1)S(1)}, bf16[32,1,18,512]{3,0,2,1:T(8,128)(2,1)S(1)}, u32[]{:S(2)}, u32[]{:S(2)}) collective-permute-start(bf16[32,1,18,512]{3,0,2,1:T(8,128)(2,1)S(1)} %get-tuple-element.10), channel_id=1, source_target_pairs={{0,224},{4,228},{8,232},{12,236},{16,240},{20,244},{24,248},{28,25... | collective-permute-start | bytes 1769480 | tf_op jit(solution)/shard_map/ppermute | solution.py:12
  52.3 2.9 %copy-start.2 = (bf16[16,96,1,1]{1,0,2,3:T(8,128)(2,1)S(1)}, bf16[16,96,1,1]{1,0,2,3:T(8,128)(2,1)}, u32[]{:S(2)}) copy-start(bf16[16,96,1,1]{1,0,2,3:T(8,128)(2,1)} %reshape.80) | copy-start | bytes 9220
  52.3 3.5 %copy-start.3 = (bf16[16,96,1,1]{1,0,2,3:T(8,128)(2,1)S(1)}, bf16[16,96,1,1]{1,0,2,3:T(8,128)(2,1)}, u32[]{:S(2)}) copy-start(bf16[16,96,1,1]{1,0,2,3:T(8,128)(2,1)} %reshape.79) | copy-start | bytes 9220
  55.2 1.1 copy-start.4
  55.2 1.6 copy-start.5
  55.8 1.6 copy-start.6
  56.3 1.6 copy-start.7
  56.8 1.6 copy-start.8
  57.4 1.6 copy-start.9
  57.9 1.6 copy-start.10
  59.5 26.5 %copy-start.1 = (bf16[3,3,3,16,64]{4,3,2,1,0:T(8,128)(2,1)S(1)}, bf16[3,3,3,16,64]{4,3,2,1,0:T(8,128)(2,1)}, u32[]{:S(2)}) copy-start(bf16[3,3,3,16,64]{4,3,2,1,0:T(8,128)(2,1)} %param.5) | copy-start | bytes 165892
  60.2 9.5 %collective-permute-start.4 = (bf16[16,2,1,512]{3,0,2,1:T(8,128)(2,1)S(1)}, bf16[16,2,1,512]{3,0,2,1:T(8,128)(2,1)S(1)}, u32[]{:S(2)}, u32[]{:S(2)}) collective-permute-start(bf16[16,2,1,512]{3,0,2,1:T(8,128)(2,1)S(1)} %get-tuple-element.15), channel_id=1, source_target_pairs={{0,4},{4,8},{8,12},{12,16},{16,20},{20,24},{24,28},{28,32},{32,36}... | collective-permute-start | bytes 98312 | tf_op jit(solution)/shard_map/ppermute | solution.py:12
  64.1 5.6 %collective-permute-start.5 = (bf16[16,2,1,512]{3,0,2,1:T(8,128)(2,1)S(1)}, bf16[16,2,1,512]{3,0,2,1:T(8,128)(2,1)S(1)}, u32[]{:S(2)}, u32[]{:S(2)}) collective-permute-start(bf16[16,2,1,512]{3,0,2,1:T(8,128)(2,1)S(1)} %get-tuple-element.16), channel_id=1, source_target_pairs={{0,252},{4,0},{8,4},{12,8},{16,12},{20,16},{24,20},{28,24},{32,28}... | collective-permute-start | bytes 98312 | tf_op jit(solution)/shard_map/ppermute | solution.py:12
  69.8 9.4 %collective-permute-start.6 = (bf16[16,1,18,512]{3,0,2,1:T(8,128)(2,1)S(1)}, bf16[16,1,18,512]{3,0,2,1:T(8,128)(2,1)S(1)}, u32[]{:S(2)}, u32[]{:S(2)}) collective-permute-start(bf16[16,1,18,512]{3,0,2,1:T(8,128)(2,1)S(1)} %get-tuple-element.13), channel_id=1, source_target_pairs={{0,32},{4,36},{8,40},{12,44},{16,48},{20,52},{24,56},{28,60},{32,6... | collective-permute-start | bytes 884744 | tf_op jit(solution)/shard_map/ppermute | solution.py:12
  69.9 14.8 %collective-permute-start.7 = (bf16[16,1,18,512]{3,0,2,1:T(8,128)(2,1)S(1)}, bf16[16,1,18,512]{3,0,2,1:T(8,128)(2,1)S(1)}, u32[]{:S(2)}, u32[]{:S(2)}) collective-permute-start(bf16[16,1,18,512]{3,0,2,1:T(8,128)(2,1)S(1)} %get-tuple-element.14), channel_id=1, source_target_pairs={{0,224},{4,228},{8,232},{12,236},{16,240},{20,244},{24,248},{28,25... | collective-permute-start | bytes 884744 | tf_op jit(solution)/shard_map/ppermute | solution.py:12
  141.6 9.1 %copy-start = (bf16[64,4,18,512]{3,0,2,1:T(8,128)(2,1)S(1)}, bf16[64,4,18,512]{3,0,2,1:T(8,128)(2,1)}, u32[]{:S(2)}) copy-start(bf16[64,4,18,512]{3,0,2,1:T(8,128)(2,1)} %all-gather.2.cloned.1.call-done) | copy-start | bytes 14155780
Sparse Core Ops, SparseCore 0:
  86.1 55.3 all-gather.1
where the time goes:
time: 174 us
  waiting for transfers between devices  76.8 us (44%)
  starting transfers between devices  30.5 us (18%)
  local copies, waits for them, and re-layouts  27.9 us (16%)
  between operations  13.6 us (8%)
  matrix products  13.3 us (8%)
  other arithmetic  11.6 us (7%)
    all_gather x1, waiting for transfers between devices, local(): lax.all_gather(hidden_pad, 'chan', axis=0, tiled=True)  54.6 us
    ppermute x8, starting transfers between devices, passed_along(): return lax.ppermute(value, axis, pairs)  30.4 us
    ppermute x8, waiting for transfers between devices, passed_along(): return lax.ppermute(value, axis, pairs)  22.2 us
    dot_general x18, matrix products, correlate(): jnp.einsum('ok,kdhw->odhw', matrix, window, preferred_element_type=jnp.fl...  13.3 us
    slice x2, local copies, waits for them, and re-layouts, widen(): left_shift = jnp.concatenate([zero_col, volume_tile[..., :-1]], 3)  10.6 us
    concatenate x2, other arithmetic, widen(): return jnp.concatenate([left_shift, volume_tile, right_shift], 0)  9.59 us
    transpose x20, local copies, waits for them, and re-layouts, correlate(): filters[depth_tap, height_tap].transpose(1, 0, 2).reshape(out_count, -1)  7.27 us
    reshape x18, local copies, waits for them, and re-layouts, correlate(): filters[depth_tap, height_tap].transpose(1, 0, 2).reshape(out_count, -1)  6.94 us
  transfers between devices with their start and end apart: 9, of which 7 were waited for; matrix products, arithmetic and copies ran while one was open for 8% of the time, Pallas kernels for 0%

commit v1 on v0

--- a/solution.py
+++ b/solution.py
@@ -4,6 +4,18 @@
 from jax.sharding import PartitionSpec as P
 
 GH = 8
+
+
+def yards_supply_all(array_here, mesh_dim="chan"):
+    return jnp.concatenate(
+        lax.all_to_all(
+            jnp.stack([array_here] * lax.axis_size(mesh_dim), axis=0),
+            axis_name=mesh_dim,
+            concat_axis=0,
+            split_axis=0,
+        ),
+        0,
+    )
 
 
 def passed_along(value, axis, steps):
@@ -92,12 +104,7 @@
         jnp.bfloat16
     )
     hidden_pad = tile_border(hidden, hidden_above, hidden_below, hidden_front, hidden_back)
-    summed = correlate(
-        widen(lax.all_gather(hidden_pad, "chan", axis=0, tiled=True)),
-        second_filters,
-        depth_rows,
-        height_rows,
-    )
+    summed = correlate(widen(yards_supply_all(hidden_pad)), second_filters, depth_rows, height_rows)
     return jax.nn.relu(summed).astype(jnp.bfloat16)
 
 

time: 174 us -> 167 us (0.960)
  between operations: 13.6 us -> 0.26 us
  starting transfers between devices: 30.5 us -> 37.9 us
  waiting for transfers between devices: 76.8 us -> 74 us
  local copies, waits for them, and re-layouts: 27.9 us -> 30.2 us
    all_gather x1 -> x0, waiting for transfers between devices: 54.6 us -> none  [local(): lax.all_gather(hidden_pad, 'chan', axis=0, tiled=True)]
    all_to_all x0 -> x1, waiting for transfers between devices: none -> 51.6 us  [yards_supply_all(): lax.all_to_all(jnp.stack([array_here] * lax.axis_size(mesh_dim), axis=0),...]
    all_to_all x0 -> x1, starting transfers between devices: none -> 7.44 us  [yards_supply_all(): lax.all_to_all(jnp.stack([array_here] * lax.axis_size(mesh_dim), axis=0),...]
    slice x2, local copies, waits for them, and re-layouts: 10.6 us -> 7.23 us  [widen(): left_shift = jnp.concatenate([zero_col, volume_tile[..., :-1]], 3)]
    all_to_all x0 -> x1, local copies, waits for them, and re-layouts: none -> 2.86 us  [yards_supply_all(): lax.all_to_all(jnp.stack([array_here] * lax.axis_size(mesh_dim), axis=0),...]
    another operation x0 -> x1, local copies, waits for them, and re-layouts: none -> 2.83 us  [yards_supply_all(): jnp.stack([array_here] * lax.axis_size(mesh_dim), axis=0)]
  transfers between devices with their start and end apart: 9 -> 9, of which waited for: 7 -> 7; matrix products, arithmetic and copies ran while one was open for 8% -> 9% of each run, Pallas kernels for 0% -> 0%
where the time goes in v1:
time: 167 us; the launch traced here: 166 us
  waiting for transfers between devices  74 us (44%)
  starting transfers between devices  37.9 us (23%)
  local copies, waits for them, and re-layouts  30.2 us (18%)
  matrix products  13.3 us (8%)
  other arithmetic  10.6 us (6%)
    all_to_all x1, waiting for transfers between devices, yards_supply_all(): lax.all_to_all(jnp.stack([array_here] * lax.axis_size(mesh_dim), axis=0),...  51.6 us
    ppermute x8, starting transfers between devices, passed_along(): return lax.ppermute(value, axis, pairs)  30.4 us
    ppermute x8, waiting for transfers between devices, passed_along(): return lax.ppermute(value, axis, pairs)  22.4 us
    dot_general x18, matrix products, correlate(): jnp.einsum('ok,kdhw->odhw', matrix, window, preferred_element_type=jnp.fl...  13.3 us
    concatenate x2, other arithmetic, widen(): return jnp.concatenate([left_shift, volume_tile, right_shift], 0)  9.59 us
    all_to_all x1, starting transfers between devices, yards_supply_all(): lax.all_to_all(jnp.stack([array_here] * lax.axis_size(mesh_dim), axis=0),...  7.44 us
    transpose x20, local copies, waits for them, and re-layouts, correlate(): filters[depth_tap, height_tap].transpose(1, 0, 2).reshape(out_count, -1)  7.26 us
    slice x2, local copies, waits for them, and re-layouts, widen(): left_shift = jnp.concatenate([zero_col, volume_tile[..., :-1]], 3)  7.23 us
  transfers between devices with their start and end apart: 9, of which 7 were waited for; matrix products, arithmetic and copies ran while one was open for 9% of the time, Pallas kernels for 0%

profile of v1, /device:TPU:1, one launch (start us, length us, event | category | flops | bytes accessed | tf_op | source)
XLA Modules:
  0.0 166.1 jit_solution(13487228163857779144)
XLA Ops:
  0.0 1.8 %copy.48 = bf16[32,2,16,512]{3,0,2,1:T(8,128)(2,1)S(1)} copy(bf16[32,2,16,512]{3,2,1,0:T(8,128)(2,1)} %param.3) | data formatting | bytes 2097152 | tf_op args[0]
  1.8 3.9 %collective-permute-start = (bf16[32,2,1,512]{3,0,2,1:T(8,128)(2,1)S(1)}, bf16[32,2,1,512]{3,0,2,1:T(8,128)(2,1)S(1)}, u32[]{:S(2)}, u32[]{:S(2)}) collective-permute-start(bf16[32,2,1,512]{3,0,2,1:T(8,128)(2,1)S(1)} %get-tuple-element.11), channel_id=1, source_target_pairs={{0,4},{4,8},{8,12},{12,16},{16,20},{20,24},{24,28},{28,32},{32,36}... | collective-permute-start | bytes 196616 | tf_op jit(solution)/shard_map/ppermute | solution.py:24
  5.7 7.8 %collective-permute-start.1 = (bf16[32,2,1,512]{3,0,2,1:T(8,128)(2,1)S(1)}, bf16[32,2,1,512]{3,0,2,1:T(8,128)(2,1)S(1)}, u32[]{:S(2)}, u32[]{:S(2)}) collective-permute-start(bf16[32,2,1,512]{3,0,2,1:T(8,128)(2,1)S(1)} %get-tuple-element.12), channel_id=1, source_target_pairs={{0,252},{4,0},{8,4},{12,8},{16,12},{20,16},{24,20},{28,24},{32,28}... | collective-permute-start | bytes 196616 | tf_op jit(solution)/shard_map/ppermute | solution.py:24
  13.5 1.7 %collective-permute-done = bf16[32,2,1,512]{3,0,2,1:T(8,128)(2,1)S(1)} collective-permute-done((bf16[32,2,1,512]{3,0,2,1:T(8,128)(2,1)S(1)}, bf16[32,2,1,512]{3,0,2,1:T(8,128)(2,1)S(1)}, u32[]{:S(2)}, u32[]{:S(2)}) %collective-permute-start) | collective-permute-done | bytes 65568 | tf_op jit(solution)/shard_map/ppermute | solution.py:24
  16.0 4.6 %collective-permute-start.3 = (bf16[32,1,18,512]{3,0,2,1:T(8,128)(2,1)S(1)}, bf16[32,1,18,512]{3,0,2,1:T(8,128)(2,1)S(1)}, u32[]{:S(2)}, u32[]{:S(2)}) collective-permute-start(bf16[32,1,18,512]{3,0,2,1:T(8,128)(2,1)S(1)} %get-tuple-element.10), channel_id=1, source_target_pairs={{0,224},{4,228},{8,232},{12,236},{16,240},{20,244},{24,248},{28,25... | collective-permute-start | bytes 1769480 | tf_op jit(solution)/shard_map/ppermute | solution.py:24
  20.6 1.5 slice_bitcast_fusion.17
  33.9 5.7 %collective-permute-done.2 = bf16[32,1,18,512]{3,0,2,1:T(8,128)(2,1)S(1)} collective-permute-done((bf16[32,1,18,512]{3,0,2,1:T(8,128)(2,1)S(1)}, bf16[32,1,18,512]{3,0,2,1:T(8,128)(2,1)S(1)}, u32[]{:S(2)}, u32[]{:S(2)}) %collective-permute-start.2) | collective-permute-done | bytes 589856 | tf_op jit(solution)/shard_map/ppermute | solution.py:24
  39.7 4.0 %collective-permute-done.3 = bf16[32,1,18,512]{3,0,2,1:T(8,128)(2,1)S(1)} collective-permute-done((bf16[32,1,18,512]{3,0,2,1:T(8,128)(2,1)S(1)}, bf16[32,1,18,512]{3,0,2,1:T(8,128)(2,1)S(1)}, u32[]{:S(2)}, u32[]{:S(2)}) %collective-permute-start.3) | collective-permute-done | bytes 589856 | tf_op jit(solution)/shard_map/ppermute | solution.py:24
  44.1 1.6 fusion.129
  45.7 2.9 %fusion.6 = bf16[96,4,18,512]{3,0,2,1:T(8,128)(2,1)S(1)} fusion(bf16[32,4,18,511]{3,0,2,1:T(8,128)(2,1)S(1)} %get-tuple-element.8, bf16[32,4,18,511]{3,0,2,1:T(8,128)(2,1)S(1)} %get-tuple-element.7, bf16[32,1,18,512]{3,0,2,1:T(8,128)(2,1)S(1)} %broadcast_select_fusion, bf16[32,2,1,512]{3,0,2,1:T(8,128)(2,1)S(1)} %broadcast_select_fusion.4, ...), kind=kLoop, calls=%fused_computation.10 | loop fusion | flops 63700992 | bytes 14146560 | tf_op jit(solution)/shard_map/concatenate | solution.py:31
  53.6 4.0 %collective-permute-start.4 = (bf16[16,2,1,512]{3,0,2,1:T(8,128)(2,1)S(1)}, bf16[16,2,1,512]{3,0,2,1:T(8,128)(2,1)S(1)}, u32[]{:S(2)}, u32[]{:S(2)}) collective-permute-start(bf16[16,2,1,512]{3,0,2,1:T(8,128)(2,1)S(1)} %get-tuple-element.15), channel_id=1, source_target_pairs={{0,4},{4,8},{8,12},{12,16},{16,20},{20,24},{24,28},{28,32},{32,36}... | collective-permute-start | bytes 98312 | tf_op jit(solution)/shard_map/ppermute | solution.py:24
  57.6 4.3 %collective-permute-start.5 = (bf16[16,2,1,512]{3,0,2,1:T(8,128)(2,1)S(1)}, bf16[16,2,1,512]{3,0,2,1:T(8,128)(2,1)S(1)}, u32[]{:S(2)}, u32[]{:S(2)}) collective-permute-start(bf16[16,2,1,512]{3,0,2,1:T(8,128)(2,1)S(1)} %get-tuple-element.16), channel_id=1, source_target_pairs={{0,252},{4,0},{8,4},{12,8},{16,12},{20,16},{24,20},{28,24},{32,28}... | collective-permute-start | bytes 98312 | tf_op jit(solution)/shard_map/ppermute | solution.py:24
  61.9 1.2 collective-permute-done.4
  63.6 5.1 %collective-permute-start.7 = (bf16[16,1,18,512]{3,0,2,1:T(8,128)(2,1)S(1)}, bf16[16,1,18,512]{3,0,2,1:T(8,128)(2,1)S(1)}, u32[]{:S(2)}, u32[]{:S(2)}) collective-permute-start(bf16[16,1,18,512]{3,0,2,1:T(8,128)(2,1)S(1)} %get-tuple-element.14), channel_id=1, source_target_pairs={{0,224},{4,228},{8,232},{12,236},{16,240},{20,244},{24,248},{28,25... | collective-permute-start | bytes 884744 | tf_op jit(solution)/shard_map/ppermute | solution.py:24
  68.6 4.2 %collective-permute-done.6 = bf16[16,1,18,512]{3,0,2,1:T(8,128)(2,1)S(1)} collective-permute-done((bf16[16,1,18,512]{3,0,2,1:T(8,128)(2,1)S(1)}, bf16[16,1,18,512]{3,0,2,1:T(8,128)(2,1)S(1)}, u32[]{:S(2)}, u32[]{:S(2)}) %collective-permute-start.6) | collective-permute-done | bytes 294944 | tf_op jit(solution)/shard_map/ppermute | solution.py:24
  72.9 5.5 %collective-permute-done.7 = bf16[16,1,18,512]{3,0,2,1:T(8,128)(2,1)S(1)} collective-permute-done((bf16[16,1,18,512]{3,0,2,1:T(8,128)(2,1)S(1)}, bf16[16,1,18,512]{3,0,2,1:T(8,128)(2,1)S(1)}, u32[]{:S(2)}, u32[]{:S(2)}) %collective-permute-start.7) | collective-permute-done | bytes 294944 | tf_op jit(solution)/shard_map/ppermute | solution.py:24
  78.6 2.8 %stack.2 = bf16[4,16,4,18,512]{4,1,3,2,0:T(8,128)(2,1)} broadcast(bf16[16,4,18,512]{3,0,2,1:T(8,128)(2,1)S(1)} %pad_maximum_fusion.2), dimensions={1,2,3,4} | broadcast | bytes 5898240 | tf_op jit(solution)/shard_map/stack | solution.py:12
  81.4 7.4 %all-to-all-start = ((bf16[4,16,4,18,512]{4,1,3,2,0:T(8,128)(2,1)}), bf16[4,16,4,18,512]{4,1,3,2,0:T(8,128)(2,1)}, u32[]{:S(2)}, u32[]{:S(2)}) async-start(bf16[4,16,4,18,512]{4,1,3,2,0:T(8,128)(2,1)} %stack.2), calls=%async_computation | async-start | bytes 9437184 | tf_op jit(solution)/shard_map/all_to_all | solution.py:11
  89.8 51.6 %all-to-all-done = bf16[4,16,4,18,512]{4,1,3,2,0:T(8,128)(2,1)} async-done(((bf16[4,16,4,18,512]{4,1,3,2,0:T(8,128)(2,1)}), bf16[4,16,4,18,512]{4,1,3,2,0:T(8,128)(2,1)}, u32[]{:S(2)}, u32[]{:S(2)}) %all-to-all-start) | async-done | bytes 4718624 | tf_op jit(solution)/shard_map/all_to_all | solution.py:11
  141.4 2.9 %copy.60 = bf16[4,16,4,18,512]{4,1,0,3,2:T(8,128)(2,1)S(1)} copy(bf16[4,16,4,18,512]{4,1,3,2,0:T(8,128)(2,1)} %all-to-all-done) | data formatting | bytes 9437184 | tf_op jit(solution)/shard_map/all_to_all | solution.py:11
  144.3 5.7 %fusion.128 = (bf16[64,4,18,511]{3,0,2,1:T(8,128)(2,1)S(1)}, bf16[64,4,18,511]{3,0,2,1:T(8,128)(2,1)}) fusion(bf16[64,4,18,512]{3,0,2,1:T(8,128)(2,1)S(1)} %bitcast.131), kind=kLoop, calls=%fused_computation.118 | loop fusion | bytes 18837504 | tf_op jit(solution)/shard_map/slice | solution.py:29
  149.9 6.7 %fusion.2 = bf16[192,4,18,512]{3,0,2,1:T(8,128)(2,1)S(1)} fusion(bf16[64,4,18,511]{3,0,2,1:T(8,128)(2,1)} %get-tuple-element.6, bf16[64,4,18,511]{3,0,2,1:T(8,128)(2,1)S(1)} %get-tuple-element.5, bf16[64,4,18,512]{3,0,2,1:T(8,128)(2,1)S(1)} %bitcast.132), kind=kLoop, calls=%fused_computation.4 | loop fusion | flops 70778880 | bytes 28293120 | tf_op jit(solution)/shard_map/concatenate | solution.py:31
  156.6 0.9 fusion.22
  157.5 0.9 fusion.59
  158.5 0.9 fusion.62
  159.4 0.9 fusion.65
  160.4 0.9 fusion.68
  161.3 0.9 fusion.71
  162.2 0.9 fusion.74
  163.2 0.9 fusion.77
  164.1 0.9 fusion.107
  165.0 1.1 copy.70
  (86 shorter events, 19.5 us)
Async XLA Ops:
  1.8 13.3 %collective-permute-start = (bf16[32,2,1,512]{3,0,2,1:T(8,128)(2,1)S(1)}, bf16[32,2,1,512]{3,0,2,1:T(8,128)(2,1)S(1)}, u32[]{:S(2)}, u32[]{:S(2)}) collective-permute-start(bf16[32,2,1,512]{3,0,2,1:T(8,128)(2,1)S(1)} %get-tuple-element.11), channel_id=1, source_target_pairs={{0,4},{4,8},{8,12},{12,16},{16,20},{20,24},{24,28},{28,32},{32,36}... | collective-permute-start | bytes 196616 | tf_op jit(solution)/shard_map/ppermute | solution.py:24
  5.7 9.4 %collective-permute-start.1 = (bf16[32,2,1,512]{3,0,2,1:T(8,128)(2,1)S(1)}, bf16[32,2,1,512]{3,0,2,1:T(8,128)(2,1)S(1)}, u32[]{:S(2)}, u32[]{:S(2)}) collective-permute-start(bf16[32,2,1,512]{3,0,2,1:T(8,128)(2,1)S(1)} %get-tuple-element.12), channel_id=1, source_target_pairs={{0,252},{4,0},{8,4},{12,8},{16,12},{20,16},{24,20},{28,24},{32,28}... | collective-permute-start | bytes 196616 | tf_op jit(solution)/shard_map/ppermute | solution.py:24
  15.4 24.2 %collective-permute-start.2 = (bf16[32,1,18,512]{3,0,2,1:T(8,128)(2,1)S(1)}, bf16[32,1,18,512]{3,0,2,1:T(8,128)(2,1)S(1)}, u32[]{:S(2)}, u32[]{:S(2)}) collective-permute-start(bf16[32,1,18,512]{3,0,2,1:T(8,128)(2,1)S(1)} %get-tuple-element.9), channel_id=1, source_target_pairs={{0,32},{4,36},{8,40},{12,44},{16,48},{20,52},{24,56},{28,60},{32,6... | collective-permute-start | bytes 1769480 | tf_op jit(solution)/shard_map/ppermute | solution.py:24
  16.0 27.7 %collective-permute-start.3 = (bf16[32,1,18,512]{3,0,2,1:T(8,128)(2,1)S(1)}, bf16[32,1,18,512]{3,0,2,1:T(8,128)(2,1)S(1)}, u32[]{:S(2)}, u32[]{:S(2)}) collective-permute-start(bf16[32,1,18,512]{3,0,2,1:T(8,128)(2,1)S(1)} %get-tuple-element.10), channel_id=1, source_target_pairs={{0,224},{4,228},{8,232},{12,236},{16,240},{20,244},{24,248},{28,25... | collective-permute-start | bytes 1769480 | tf_op jit(solution)/shard_map/ppermute | solution.py:24
  45.7 2.9 %copy-start.1 = (bf16[16,96,1,1]{1,0,2,3:T(8,128)(2,1)S(1)}, bf16[16,96,1,1]{1,0,2,3:T(8,128)(2,1)}, u32[]{:S(2)}) copy-start(bf16[16,96,1,1]{1,0,2,3:T(8,128)(2,1)} %reshape.86) | copy-start | bytes 9220
  45.7 3.5 %copy-start.2 = (bf16[16,96,1,1]{1,0,2,3:T(8,128)(2,1)S(1)}, bf16[16,96,1,1]{1,0,2,3:T(8,128)(2,1)}, u32[]{:S(2)}) copy-start(bf16[16,96,1,1]{1,0,2,3:T(8,128)(2,1)} %reshape.85) | copy-start | bytes 9220
  48.7 1.1 copy-start.3
  48.7 1.6 copy-start.4
  49.2 1.6 copy-start.5
  49.8 1.6 copy-start.6
  50.3 1.6 copy-start.7
  50.8 1.6 copy-start.8
  51.4 1.6 copy-start.9
  53.6 9.5 %collective-permute-start.4 = (bf16[16,2,1,512]{3,0,2,1:T(8,128)(2,1)S(1)}, bf16[16,2,1,512]{3,0,2,1:T(8,128)(2,1)S(1)}, u32[]{:S(2)}, u32[]{:S(2)}) collective-permute-start(bf16[16,2,1,512]{3,0,2,1:T(8,128)(2,1)S(1)} %get-tuple-element.15), channel_id=1, source_target_pairs={{0,4},{4,8},{8,12},{12,16},{16,20},{20,24},{24,28},{28,32},{32,36}... | collective-permute-start | bytes 98312 | tf_op jit(solution)/shard_map/ppermute | solution.py:24
  57.6 5.6 %collective-permute-start.5 = (bf16[16,2,1,512]{3,0,2,1:T(8,128)(2,1)S(1)}, bf16[16,2,1,512]{3,0,2,1:T(8,128)(2,1)S(1)}, u32[]{:S(2)}, u32[]{:S(2)}) collective-permute-start(bf16[16,2,1,512]{3,0,2,1:T(8,128)(2,1)S(1)} %get-tuple-element.16), channel_id=1, source_target_pairs={{0,252},{4,0},{8,4},{12,8},{16,12},{20,16},{24,20},{28,24},{32,28}... | collective-permute-start | bytes 98312 | tf_op jit(solution)/shard_map/ppermute | solution.py:24
  63.3 9.5 %collective-permute-start.6 = (bf16[16,1,18,512]{3,0,2,1:T(8,128)(2,1)S(1)}, bf16[16,1,18,512]{3,0,2,1:T(8,128)(2,1)S(1)}, u32[]{:S(2)}, u32[]{:S(2)}) collective-permute-start(bf16[16,1,18,512]{3,0,2,1:T(8,128)(2,1)S(1)} %get-tuple-element.13), channel_id=1, source_target_pairs={{0,32},{4,36},{8,40},{12,44},{16,48},{20,52},{24,56},{28,60},{32,6... | collective-permute-start | bytes 884744 | tf_op jit(solution)/shard_map/ppermute | solution.py:24
  63.6 14.8 %collective-permute-start.7 = (bf16[16,1,18,512]{3,0,2,1:T(8,128)(2,1)S(1)}, bf16[16,1,18,512]{3,0,2,1:T(8,128)(2,1)S(1)}, u32[]{:S(2)}, u32[]{:S(2)}) collective-permute-start(bf16[16,1,18,512]{3,0,2,1:T(8,128)(2,1)S(1)} %get-tuple-element.14), channel_id=1, source_target_pairs={{0,224},{4,228},{8,232},{12,236},{16,240},{20,244},{24,248},{28,25... | collective-permute-start | bytes 884744 | tf_op jit(solution)/shard_map/ppermute | solution.py:24
  78.6 10.3 %copy-start = (bf16[3,3,3,16,64]{4,3,2,1,0:T(8,128)(2,1)S(1)}, bf16[3,3,3,16,64]{4,3,2,1,0:T(8,128)(2,1)}, u32[]{:S(2)}) copy-start(bf16[3,3,3,16,64]{4,3,2,1,0:T(8,128)(2,1)} %param.5) | copy-start | bytes 165892
  81.4 60.0 %all-to-all-start = ((bf16[4,16,4,18,512]{4,1,3,2,0:T(8,128)(2,1)}), bf16[4,16,4,18,512]{4,1,3,2,0:T(8,128)(2,1)}, u32[]{:S(2)}, u32[]{:S(2)}) async-start(bf16[4,16,4,18,512]{4,1,3,2,0:T(8,128)(2,1)} %stack.2), calls=%async_computation | async-start | bytes 9437184 | tf_op jit(solution)/shard_map/all_to_all | solution.py:11
